TPU v7x, 256 devices: a whole 4x4x8 slice. The times are simulated.
256 devices in a mesh: facet: 8 (over z), chan: 32 (over y, x, core).
Axes of the slice: x: 4, y: 4, z: 8, core: 2. Of those that a mesh axis runs over, the one named last changes fastest.
Arguments:
- sky_image: float32 [256, 32, 4096], P('chan', 'facet'), may hold values from -100 to 100
- dual_field: float32 [256, 32, 4096], P(None, 'facet', 'chan'), may hold values from -100 to 100
- sketch_matrix: bfloat16 [32, 4096, 128], P('facet', 'chan'), may hold values from -0.046875 to 0.046875
- grid_tiles: float32 [256, 4, 128, 128], P('chan'), may hold values from -0.5 to 0.5
- freq_block: int32 [256, 4], P('chan'), may hold values from 0 to 31
- vis_block: int32 [256, 4], P('chan'), may hold values from 0 to 3
- vis_data: float32 [256, 2, 32, 4, 128], P('chan', None, 'facet'), may hold values from -6 to 6
Outputs:
- new_image: float32 [256, 32, 4096], P('chan', 'facet')
- new_dual: float32 [256, 32, 4096], P(None, 'facet', 'chan')
All inputs are finite; a program needn't handle non-finite values.
Results may differ from a plain program's by a relative error of at most 0.0003.
Values sent between devices are 32-bit elements; how exact they have to be, the bound alone decides.
No kernel may reach another device: no remote copies, remote signals or barrier semaphores. Data moves between devices by JAX's collectives and lax.ppermute only.
A program may use at most 128 MiB of HBM per device.

v0:
```python
import math
import jax
import jax.numpy as jnp
from jax import lax
from jax.sharding import PartitionSpec as P

SIGN_ITERS = 12
ROOT_ITERS = 14
step_primal = 0.4
smooth_weight = 0.25
step_dual = 0.5
shrink_ratio = 0.25


def padded_2(block, sides, width):
    for axis, dim in sides:
        count = lax.axis_size(axis)
        forward = [(i, i + 1) for i in range(count - 1)]
        backward = [(target, source) for source, target in forward]
        low = lax.ppermute(
            lax.slice_in_dim(block, block.shape[dim] - width, None, axis=dim), axis, forward
        )
        high = lax.ppermute(lax.slice_in_dim(block, 0, width, axis=dim), axis, backward)
        block = jnp.concatenate([low, block, high], axis=dim)
    return block


def matmul_hi(first_mat, second_mat):
    return jnp.dot(first_mat, second_mat, precision=lax.Precision.HIGHEST)


def shrink_matrix(gram_mat):
    order_n = gram_mat.shape[0]
    identity = jnp.eye(order_n, dtype=gram_mat.dtype)
    thresh_sq = shrink_ratio * jnp.trace(gram_mat) / order_n
    shifted = gram_mat - thresh_sq * identity
    signum = shifted / jnp.sqrt(jnp.sum(shifted * shifted))

    def sign_step(turn_no, current):
        return 1.5 * current - 0.5 * matmul_hi(matmul_hi(current, current), current)

    signum = lax.fori_loop(0, SIGN_ITERS, sign_step, signum)
    keeper = 0.5 * (identity + signum)
    floored = 0.5 * (gram_mat + thresh_sq * identity + matmul_hi(shifted, signum))
    scale_c = jnp.sqrt(jnp.sum(floored * floored))

    def root_step(turn_no, state_pair):
        root_iter, inv_iter = state_pair
        step_mat = 0.5 * (3.0 * identity - matmul_hi(inv_iter, root_iter))
        return (matmul_hi(root_iter, step_mat), matmul_hi(step_mat, inv_iter))

    root_iter, inv_iter = lax.fori_loop(0, ROOT_ITERS, root_step, (floored / scale_c, identity))
    inv_root = inv_iter / jnp.sqrt(scale_c)
    return matmul_hi(keeper, identity - jnp.sqrt(thresh_sq) * inv_root)


def basis_from(sketch):
    lower_fac = jnp.linalg.cholesky(matmul_hi(sketch.T, sketch))
    return jax.scipy.linalg.solve_triangular(lower_fac, sketch.T, lower=True).T


def phase_pair(count_a, count_b, period):
    first_idx = lax.broadcasted_iota(jnp.int32, (count_a, count_b), 0)
    second_idx = lax.broadcasted_iota(jnp.int32, (count_a, count_b), 1)
    angle_grid = 2.0 * math.pi / period * (first_idx * second_idx % period).astype(jnp.float32)
    return (jnp.cos(angle_grid), jnp.sin(angle_grid))


def spectrum_tables(width, block):
    blocks_n = width // block
    cos_a, sin_a = phase_pair(blocks_n, blocks_n, blocks_n)
    cos_b, sin_b = phase_pair(block, block, block)
    cos_t, sin_t = phase_pair(blocks_n, block, width)
    return (cos_a, sin_a, cos_b, sin_b, cos_t, sin_t)


def forward_rows(rows_img, tables, block):
    cos_a, sin_a, cos_b, sin_b, cos_t, sin_t = tables
    row_count, width = rows_img.shape
    blocks_n = width // block
    hi = lax.Precision.HIGHEST
    blocks = rows_img.reshape(row_count, blocks_n, block)
    part_re = jnp.einsum("kn,bnm->bkm", cos_a, blocks, precision=hi)
    part_im = -jnp.einsum("kn,bnm->bkm", sin_a, blocks, precision=hi)
    turned_re = (part_re * cos_t + part_im * sin_t).reshape(-1, block)
    turned_im = (part_im * cos_t - part_re * sin_t).reshape(-1, block)
    ortho_scale = 1.0 / math.sqrt(width)
    spec_re = (matmul_hi(turned_re, cos_b) + matmul_hi(turned_im, sin_b)) * ortho_scale
    spec_im = (matmul_hi(turned_im, cos_b) - matmul_hi(turned_re, sin_b)) * ortho_scale
    return (
        spec_re.reshape(row_count, blocks_n, block),
        spec_im.reshape(row_count, blocks_n, block),
    )


def adjoint_rows(spec_re, spec_im, tables):
    cos_a, sin_a, cos_b, sin_b, cos_t, sin_t = tables
    row_count, blocks_n, block = spec_re.shape
    hi = lax.Precision.HIGHEST
    flat_re = spec_re.reshape(-1, block)
    flat_im = spec_im.reshape(-1, block)
    back_re = (matmul_hi(flat_re, cos_b) - matmul_hi(flat_im, sin_b)).reshape(
        row_count, blocks_n, block
    )
    back_im = (matmul_hi(flat_im, cos_b) + matmul_hi(flat_re, sin_b)).reshape(
        row_count, blocks_n, block
    )
    turn_re = back_re * cos_t - back_im * sin_t
    turn_im = back_re * sin_t + back_im * cos_t
    rows_out = jnp.einsum("kn,bkm->bnm", cos_a, turn_re, precision=hi) - jnp.einsum(
        "kn,bkm->bnm", sin_a, turn_im, precision=hi
    )
    width = blocks_n * block
    return rows_out.reshape(row_count, width) * (1.0 / math.sqrt(width))


def data_gradient(sky_image, grid_tiles, freq_block, vis_block, vis_data):
    chan_count, row_count, width = sky_image.shape
    block = grid_tiles.shape[2]
    blocks_n = width // block
    hi = lax.Precision.HIGHEST
    tables = spectrum_tables(width, block)
    columns = lax.all_to_all(sky_image, "facet", split_axis=2, concat_axis=1, tiled=True)
    all_rows = columns.shape[1]
    cos_c, sin_c = phase_pair(all_rows, all_rows, all_rows)
    column_scale = 1.0 / math.sqrt(all_rows)
    column_re = jnp.einsum("pq,cqn->cpn", cos_c, columns, precision=hi) * column_scale
    column_im = -jnp.einsum("pq,cqn->cpn", sin_c, columns, precision=hi) * column_scale
    column_spec = jnp.stack([column_re, column_im], 1)
    row_spec = lax.all_to_all(column_spec, "facet", split_axis=2, concat_axis=3, tiled=True)
    four_re, four_im = forward_rows(
        row_spec.reshape(chan_count * 2 * row_count, width), tables, block
    )
    four_re = four_re.reshape(chan_count, 2, row_count, blocks_n, block)
    four_im = four_im.reshape(chan_count, 2, row_count, blocks_n, block)
    spec_re = four_re[:, 0] - four_im[:, 1]
    spec_im = four_im[:, 0] + four_re[:, 1]
    spectra = jnp.stack([spec_re, spec_im], 1)
    pick_onehot = jax.nn.one_hot(freq_block, blocks_n, dtype=jnp.float32)
    place_onehot = jax.nn.one_hot(vis_block, vis_data.shape[3], dtype=jnp.float32)
    chosen = jnp.einsum("ctb,cxrbk->cxtrk", pick_onehot, spectra, precision=hi)
    products = jnp.einsum("cxtrk,ctkm->cxtrm", chosen, grid_tiles, precision=hi)
    predicted = jnp.einsum("ctv,cxtrm->cxrvm", place_onehot, products, precision=hi)
    residual = predicted - vis_data
    spread = jnp.einsum("ctv,cxrvm->cxtrm", place_onehot, residual, precision=hi)
    pulled = jnp.einsum("cxtrm,ctkm->cxtrk", spread, grid_tiles, precision=hi)
    back_spec = jnp.einsum("ctb,cxtrk->cxrbk", pick_onehot, pulled, precision=hi)
    back_re = back_spec[:, 0].reshape(-1, blocks_n, block)
    back_im = back_spec[:, 1].reshape(-1, blocks_n, block)
    inverted = adjoint_rows(
        jnp.concatenate([back_re, back_im], 0), jnp.concatenate([back_im, -back_re], 0), tables
    )
    inverted = jnp.swapaxes(inverted.reshape(2, chan_count, row_count, width), 0, 1)
    spatial = lax.all_to_all(inverted, "facet", split_axis=3, concat_axis=2, tiled=True)
    gradient_cols = (
        jnp.einsum("pq,cpn->cqn", cos_c, spatial[:, 0], precision=hi)
        - jnp.einsum("pq,cpn->cqn", sin_c, spatial[:, 1], precision=hi)
    ) * column_scale
    return lax.all_to_all(gradient_cols, "facet", split_axis=1, concat_axis=2, tiled=True)


def take_sketch(pixels, sketch_rows):
    return jnp.einsum("crw,rwk->ck", pixels, sketch_rows, precision=lax.Precision.HIGHEST)


def project_rows(basis_mat, pixels):
    return jnp.einsum("ck,crw->krw", basis_mat, pixels, precision=lax.Precision.HIGHEST)


def on_device(sky_image, dual_field, sketch_matrix, grid_tiles, freq_block, vis_block, vis_data):
    hi = lax.Precision.HIGHEST
    dual_chan = lax.all_to_all(dual_field, "chan", split_axis=0, concat_axis=2, tiled=True)
    padded = padded_2(sky_image, (("facet", 1),), 1)
    gradient = data_gradient(sky_image, grid_tiles, freq_block, vis_block, vis_data)
    smooth = 2.0 * sky_image - padded[:, :-2] - padded[:, 2:]
    new_image = sky_image - step_primal * (gradient + smooth_weight * smooth + dual_chan)
    merged = dual_chan + step_dual * (2.0 * new_image - sky_image)
    sketch_rows = sketch_matrix.astype(jnp.float32)
    pixels = lax.all_to_all(merged, "chan", split_axis=2, concat_axis=0, tiled=True)
    sketch = lax.psum(take_sketch(pixels, sketch_rows), "chan")
    basis_mat = basis_from(sketch)
    coords = project_rows(basis_mat, pixels)
    gram_mat = lax.psum(jnp.einsum("krw,jrw->kj", coords, coords, precision=hi), "chan")
    shrink = shrink_matrix(gram_mat)
    new_dual = pixels - jnp.einsum(
        "ck,krw->crw", matmul_hi(basis_mat, shrink), coords, precision=hi
    )
    return (new_image, new_dual)


def solution(mesh):
    placed = (
        P("chan", "facet", None),
        P(None, "facet", "chan"),
        P("facet", "chan", None),
        P("chan", None, None, None),
        P("chan", None),
        P("chan", None),
        P("chan", None, "facet", None, None),
    )
    return jax.shard_map(
        on_device,
        mesh=mesh,
        in_specs=placed,
        out_specs=(P("chan", "facet", None), P(None, "facet", "chan")),
        check_vma=False,
    )
```

profile of v0, /device:TPU:1, one launch (start us, length us, event | category | flops | bytes accessed | tf_op | source)
XLA Modules:
  0.0 629.0 jit_solution(11363027889808603613)
XLA Ops:
  7.2 6.9 %copy.95 = f32[8,4,4096]{0,1,2:T(4,128)} copy(f32[8,4,4096]{2,1,0:T(4,128)} %param.11) | data formatting | bytes 1048576 | tf_op args[0]
  14.1 11.4 %reshape.86 = f32[8,1,16384]{2,1,0:T(1,128)S(1)} reshape(f32[4096,4,8]{2,1,0:T(4,128)} %bitcast.218) | data formatting | bytes 1048576
  25.5 25.4 %all_to_all.105 = f32[8,1,16384]{2,1,0:T(1,128)S(1)} all-to-all(f32[8,1,16384]{2,1,0:T(1,128)S(1)} %reshape.86), channel_id=1, replica_groups=mesh['facet'=8,'chan'=32] {'facet'}, dimensions={0} | all-to-all | bytes 1048576 | tf_op jit(solution)/shard_map/all_to_all | solution.py:123
  53.3 13.1 %reshape.87 = f32[4096,4,8]{2,1,0:T(4,128)} reshape(f32[8,16384]{1,0:T(8,128)S(1)} %reduce.6) | data formatting | bytes 1048576
  66.4 6.7 %copy.96 = f32[8,4,8,512]{3,1,2,0:T(4,128)S(1)} copy(f32[8,4,8,512]{0,1,3,2:T(4,128)} %bitcast.215) | data formatting | bytes 1048576 | tf_op jit(solution)/shard_map/all_to_all | solution.py:123
  76.4 3.7 all-to-all-start.1
  80.4 28.5 %all-to-all-done.1 = f32[8,2,32,512]{3,0,1,2:T(8,128)S(1)} async-done(((f32[8,2,32,512]{3,0,1,2:T(8,128)}), f32[8,2,32,512]{3,0,1,2:T(8,128)S(1)}, u32[]{:S(2)}, u32[]{:S(2)}) %all-to-all-start.1) | async-done | bytes 1048608 | tf_op jit(solution)/shard_map/all_to_all | solution.py:130
  122.5 3.8 fusion.21
  135.1 11.1 %copy.110 = f32[2,8,4,4096]{1,2,0,3:T(4,128)} copy(f32[2,8,4,4096]{3,2,1,0:T(4,128)S(1)} %mul.315) | data formatting | bytes 2097152 | tf_op jit(solution)/shard_map/mul | solution.py:114
  146.2 14.5 %bitcast_bitcast_fusion = f32[4096,2,4,8]{3,2,1,0:T(4,128)} fusion(f32[2,8,4,4096]{1,2,0,3:T(4,128)} %copy.110), kind=kLoop, calls=%fused_computation.239 | loop fusion | bytes 2097152
  160.7 21.3 %reshape.88 = f32[8,1,32768]{2,1,0:T(1,128)S(1)} reshape(f32[4096,2,4,8]{3,2,1,0:T(4,128)} %bitcast_bitcast_fusion) | data formatting | bytes 2097152
  182.0 30.5 %all_to_all.106 = f32[8,1,32768]{2,1,0:T(1,128)S(1)} all-to-all(f32[8,1,32768]{2,1,0:T(1,128)S(1)} %reshape.88), channel_id=1, replica_groups=mesh['facet'=8,'chan'=32] {'facet'}, dimensions={0} | all-to-all | bytes 2097152 | tf_op jit(solution)/shard_map/all_to_all | solution.py:154
  212.5 3.1 reduce.7
  215.7 25.6 %reshape.89 = f32[4096,2,4,8]{3,2,1,0:T(4,128)} reshape(f32[8,32768]{1,0:T(8,128)S(1)} %reduce.7) | data formatting | bytes 2097152
  241.3 13.2 %copy.111 = f32[8,2,4,8,512]{4,2,3,0,1:T(4,128)S(1)} copy(f32[8,2,4,8,512]{0,2,1,4,3:T(4,128)} %bitcast.214) | data formatting | bytes 2097152 | tf_op jit(solution)/shard_map/all_to_all | solution.py:154
  257.3 3.5 all-to-all-start.3
  261.1 16.0 %all-to-all-done.3 = f32[8,32,512]{2,0,1:T(8,128)S(1)} async-done(((f32[8,32,512]{2,0,1:T(8,128)}), f32[8,32,512]{2,0,1:T(8,128)S(1)}, u32[]{:S(2)}, u32[]{:S(2)}) %all-to-all-start.3) | async-done | bytes 524320 | tf_op jit(solution)/shard_map/all_to_all | solution.py:159
  277.2 9.2 %all-to-all-start.4 = ((f32[256,4,128]{2,1,0:T(4,128)}), f32[256,4,128]{2,1,0:T(4,128)S(1)}, u32[]{:S(2)}, u32[]{:S(2)}) async-start(f32[256,4,128]{2,1,0:T(4,128)} %param.12), calls=%async_computation.4 | async-start | bytes 1048576 | tf_op jit(solution)/shard_map/all_to_all | solution.py:172
  286.5 2.2 collective-permute-start
  291.3 3.8 collective-permute-done.1
  295.1 2.7 all-to-all-done.4
  298.3 5.9 copy.122
  304.2 11.4 %reshape.90 = f32[32,1,4096]{2,1,0:T(1,128)S(1)} reshape(f32[4096,4,8]{2,1,0:T(4,128)} %bitcast.216) | data formatting | bytes 1048576
  315.6 17.2 %all_to_all.107 = f32[32,1,4096]{2,1,0:T(1,128)S(1)} all-to-all(f32[32,1,4096]{2,1,0:T(1,128)S(1)} %reshape.90), channel_id=1, replica_groups=mesh['facet'=8,'chan'=32] {'chan'}, dimensions={0} | all-to-all | bytes 1048576 | tf_op jit(solution)/shard_map/all_to_all | solution.py:179
  334.7 11.3 %reshape.91 = f32[4096,4,8]{2,1,0:T(4,128)} reshape(f32[32,4096]{1,0:T(8,128)S(1)} %reduce.8) | data formatting | bytes 1048576
  346.0 6.7 %copy.123 = f32[8,4,32,128]{3,0,2,1:T(8,128)S(1)} copy(f32[8,4,32,128]{0,1,3,2:T(4,128)} %bitcast.217) | data formatting | bytes 1048576 | tf_op jit(solution)/shard_map/all_to_all | solution.py:179
  353.9 105.1 %all-reduce.3.cloned.1.call-done = f32[256,128]{1,0:T(8,128)} async-done(((f32[256,128]{1,0:T(8,128)}), f32[256,128]{1,0:T(8,128)}) %all-reduce.3.cloned.1.call-update) | async-done | bytes 131088 | tf_op jit(solution)/shard_map/psum | solution.py:180
  460.4 11.7 %cholesky.22 = f32[128,128]{1,0:T(8,128)S(1)} custom-call(f32[128,128]{1,0:T(8,128)S(1)} %fusion.62), custom_call_target="Cholesky" | custom-call | tf_op jit(solution)/shard_map/jit(cholesky)/cholesky | solution.py:58
  473.5 9.8 %custom-call.7 = f32[1,128,128]{1,2,0:T(8,128)S(1)} custom-call(f32[1,128,128]{2,1,0:T(8,128)S(1)} %fusion.56), custom_call_target="InvertDiagBlocksLowerTriangular" | custom-call | tf_op jit(solution)/shard_map/jit(_solve_triangular)/triangular_solve | solution.py:59
  487.1 106.4 %all-reduce.5.cloned.1.call-done = f32[128,128]{1,0:T(8,128)} async-done(((f32[128,128]{1,0:T(8,128)}), f32[128,128]{1,0:T(8,128)}) %all-reduce.5.cloned.1.call-update) | async-done | bytes 65552 | tf_op jit(solution)/shard_map/psum | solution.py:183
  598.9 5.4 while.23
  607.1 11.4 %while.24 = (s32[]{:T(128)}, f32[128,128]{0,1:T(8,128)S(1)}, f32[128,128]{1,0:T(8,128)S(1)}, s32[]{:T(128)}) while((s32[]{:T(128)}, f32[128,128]{0,1:T(8,128)S(1)}, f32[128,128]{1,0:T(8,128)S(1)}, s32[]{:T(128)}) %tuple.57), condition=%wide.region_10.11_spmd.clone, body=%wide.region_9.10_spmd.clone.sunk | while | flops 75563008 | bytes 852021 | solution.py:52
  (193 shorter events, 68.8 us)
Async XLA Ops:
  7.2 112.7 %copy-start = (f32[8,4,128,128]{3,2,1,0:T(8,128)S(1)}, f32[8,4,128,128]{3,2,1,0:T(8,128)}, u32[]{:S(2)}) copy-start(f32[8,4,128,128]{3,2,1,0:T(8,128)} %param.14) | copy-start | bytes 6291460
  66.4 13.8 %copy-start.6 = (s32[8,4]{0,1:T(4,128)S(1)}, s32[8,4]{0,1:T(4,128)}, u32[]{:S(2)}) copy-start(s32[8,4]{0,1:T(4,128)} %param.15) | copy-start | bytes 388
  66.4 13.9 %copy-start.7 = (s32[8,4]{0,1:T(4,128)S(1)}, s32[8,4]{0,1:T(4,128)}, u32[]{:S(2)}) copy-start(s32[8,4]{0,1:T(4,128)} %param.16) | copy-start | bytes 388
  76.4 32.5 %all-to-all-start.1 = ((f32[8,2,32,512]{3,0,1,2:T(8,128)}), f32[8,2,32,512]{3,0,1,2:T(8,128)S(1)}, u32[]{:S(2)}, u32[]{:S(2)}) async-start(f32[8,2,32,512]{3,0,1,2:T(8,128)} %copy.99), calls=%async_computation.1 | async-start | bytes 2097152 | tf_op jit(solution)/shard_map/all_to_all | solution.py:130
  114.2 7.5 %copy-start.4 = (f32[8,2,4,4,128]{4,3,2,1,0:T(4,128)S(1)}, f32[8,2,4,4,128]{4,3,2,1,0:T(4,128)}, u32[]{:S(2)}) copy-start(f32[8,2,4,4,128]{4,3,2,1,0:T(4,128)} %param.17) | copy-start | bytes 393220
  241.3 19.6 %copy-start.2 = (f32[8,4,4096]{2,1,0:T(4,128)S(1)}, f32[8,4,4096]{2,1,0:T(4,128)}, u32[]{:S(2)}) copy-start(f32[8,4,4096]{2,1,0:T(4,128)} %param.11) | copy-start | bytes 1572868
  257.3 19.9 %all-to-all-start.3 = ((f32[8,32,512]{2,0,1:T(8,128)}), f32[8,32,512]{2,0,1:T(8,128)S(1)}, u32[]{:S(2)}, u32[]{:S(2)}) async-start(f32[8,32,512]{2,0,1:T(8,128)} %copy.112), calls=%async_computation.3 | async-start | bytes 1048576 | tf_op jit(solution)/shard_map/all_to_all | solution.py:159
  277.2 20.7 %all-to-all-start.4 = ((f32[256,4,128]{2,1,0:T(4,128)}), f32[256,4,128]{2,1,0:T(4,128)S(1)}, u32[]{:S(2)}, u32[]{:S(2)}) async-start(f32[256,4,128]{2,1,0:T(4,128)} %param.12), calls=%async_computation.4 | async-start | bytes 1048576 | tf_op jit(solution)/shard_map/all_to_all | solution.py:172
  286.4 172.5 %all-reduce.3.cloned.1.call-start = ((), (), s32[]{:S(2)}) async-start(), calls=%async_computation.6 | async-start | bytes 262144 | tf_op jit(solution)/shard_map/psum | solution.py:180
  286.5 4.8 collective-permute-start
  288.7 6.4 %collective-permute-start.1 = (f32[8,1,4096]{2,0,1:T(8,128)S(1)}, f32[8,1,4096]{2,0,1:T(8,128)S(1)}, u32[]{:S(2)}, u32[]{:S(2)}) collective-permute-start(f32[8,1,4096]{2,0,1:T(8,128)S(1)} %get-tuple-element.85), channel_id=1, source_target_pairs={{32,0},{64,32},{96,64},{128,96},{160,128},{192,160},{224,192},{33,... | collective-permute-start | bytes 393224 | tf_op jit(solution)/shard_map/ppermute | solution.py:23
  334.7 18.1 %copy-start.5 = (bf16[4,128,128]{2,1,0:T(8,128)(2,1)S(1)}, bf16[4,128,128]{2,1,0:T(8,128)(2,1)}, u32[]{:S(2)}) copy-start(bf16[4,128,128]{2,1,0:T(8,128)(2,1)} %param.13) | copy-start | bytes 393220
  346.0 275.7 %copy-start.1 = (f32[8,4,128,128]{3,2,1,0:T(8,128)S(1)}, f32[8,4,128,128]{3,2,1,0:T(8,128)}, u32[]{:S(2)}) copy-start(f32[8,4,128,128]{3,2,1,0:T(8,128)} %param.14) | copy-start | bytes 6291460
  353.8 239.7 %all-reduce.5.cloned.1.call-start = ((), (), s32[]{:S(2)}) async-start(), calls=%async_computation.7 | async-start | bytes 131072 | tf_op jit(solution)/shard_map/psum | solution.py:183
  484.5 1.5 copy-start.3
Sparse Core Ops, SparseCore 0:
  353.9 104.9 all-reduce.2
  486.1 107.3 all-reduce.4
where the time goes:
time: 633 us; the launch traced here: 629 us
  waiting for transfers between devices  264 us (42%)
  local copies, waits for them, and re-layouts  170 us (27%)
  blocking collectives  73.1 us (12%)
  matrix products  49.3 us (8%)
  other arithmetic  34.9 us (6%)
  starting transfers between devices  20 us (3%)
  between operations  17.3 us (3%)
    unnamed x30, local copies, waits for them, and re-layouts  118 us
    psum x1, waiting for transfers between devices, on_device(): lax.psum(jnp.einsum('krw,jrw->kj', coords, coords, precision=hi), 'chan')  106 us
    psum x1, waiting for transfers between devices, on_device(): sketch = lax.psum(take_sketch(pixels, sketch_rows), 'chan')  105 us
    all_to_all x1, blocking collectives, data_gradient(): lax.all_to_all(inverted, 'facet', split_axis=3, concat_axis=2, tiled=True)  30.5 us
    dot_general x78, matrix products, matmul_hi(): return jnp.dot(first_mat, second_mat, precision=lax.Precision.HIGHEST)  29.9 us
    all_to_all x1, waiting for transfers between devices, data_gradient(): lax.all_to_all(column_spec, 'facet', split_axis=2, concat_axis=3, tiled=T...  28.5 us
    all_to_all x1, blocking collectives, data_gradient(): lax.all_to_all(sky_image, 'facet', split_axis=2, concat_axis=1, tiled=True)  25.4 us
    all_to_all x1, blocking collectives, on_device(): lax.all_to_all(merged, 'chan', split_axis=2, concat_axis=0, tiled=True)  17.2 us
  transfers between devices with their start and end apart: 7, of which 7 were waited for; matrix products, arithmetic and copies ran while one was open for 0% of the time, Pallas kernels for 0%

commit v1 on v0

--- a/solution.py
+++ b/solution.py
@@ -180,7 +180,9 @@
     sketch = lax.psum(take_sketch(pixels, sketch_rows), "chan")
     basis_mat = basis_from(sketch)
     coords = project_rows(basis_mat, pixels)
-    gram_mat = lax.psum(jnp.einsum("krw,jrw->kj", coords, coords, precision=hi), "chan")
+    gram_mat = jnp.sum(
+        lax.all_gather(jnp.einsum("krw,jrw->kj", coords, coords, precision=hi), "chan"), axis=0
+    )
     shrink = shrink_matrix(gram_mat)
     new_dual = pixels - jnp.einsum(
         "ck,krw->crw", matmul_hi(basis_mat, shrink), coords, precision=hi

time: 633 us -> 571 us (0.902)
  waiting for transfers between devices: 264 us -> 205 us
    psum x1 -> x0, waiting for transfers between devices: 106 us -> none  [on_device(): lax.psum(jnp.einsum('krw,jrw->kj', coords, coords, precision=hi), 'chan')]
    all_gather x0 -> x1, waiting for transfers between devices: none -> 47.7 us  [on_device(): lax.all_gather(jnp.einsum('krw,jrw->kj', coords, coords, precision=hi), '...]
    unnamed x30 -> x32, local copies, waits for them, and re-layouts: 118 us -> 118 us
where the time goes in v1:
time: 571 us; the launch traced here: 567 us
  waiting for transfers between devices  205 us (36%)
  local copies, waits for them, and re-layouts  169 us (30%)
  blocking collectives  73 us (13%)
  matrix products  47.6 us (8%)
  other arithmetic  33.9 us (6%)
  starting transfers between devices  19.9 us (3%)
  between operations  17.1 us (3%)
    unnamed x32, local copies, waits for them, and re-layouts  118 us
    psum x1, waiting for transfers between devices, on_device(): sketch = lax.psum(take_sketch(pixels, sketch_rows), 'chan')  105 us
    all_gather x1, waiting for transfers between devices, on_device(): lax.all_gather(jnp.einsum('krw,jrw->kj', coords, coords, precision=hi), '...  47.7 us
    all_to_all x1, blocking collectives, data_gradient(): lax.all_to_all(inverted, 'facet', split_axis=3, concat_axis=2, tiled=True)  30.5 us
    all_to_all x1, waiting for transfers between devices, data_gradient(): lax.all_to_all(column_spec, 'facet', split_axis=2, concat_axis=3, tiled=T...  28.5 us
    dot_general x78, matrix products, matmul_hi(): return jnp.dot(first_mat, second_mat, precision=lax.Precision.HIGHEST)  28.2 us
    all_to_all x1, blocking collectives, data_gradient(): lax.all_to_all(sky_image, 'facet', split_axis=2, concat_axis=1, tiled=True)  25.4 us
    all_to_all x1, blocking collectives, on_device(): lax.all_to_all(merged, 'chan', split_axis=2, concat_axis=0, tiled=True)  17.2 us
  transfers between devices with their start and end apart: 7, of which 7 were waited for; matrix products, arithmetic and copies ran while one was open for 0% of the time, Pallas kernels for 0%

profile of v1, /device:TPU:1, one launch (start us, length us, event | category | flops | bytes accessed | tf_op | source)
XLA Modules:
  0.0 567.0 jit_solution(2938320533680479425)
XLA Ops:
  7.2 6.9 %copy.95 = f32[8,4,4096]{0,1,2:T(4,128)} copy(f32[8,4,4096]{2,1,0:T(4,128)} %param.11) | data formatting | bytes 1048576 | tf_op args[0]
  14.1 11.4 %reshape.87 = f32[8,1,16384]{2,1,0:T(1,128)S(1)} reshape(f32[4096,4,8]{2,1,0:T(4,128)} %bitcast.219) | data formatting | bytes 1048576
  25.5 25.4 %all_to_all.105 = f32[8,1,16384]{2,1,0:T(1,128)S(1)} all-to-all(f32[8,1,16384]{2,1,0:T(1,128)S(1)} %reshape.87), channel_id=1, replica_groups=mesh['facet'=8,'chan'=32] {'facet'}, dimensions={0} | all-to-all | bytes 1048576 | tf_op jit(solution)/shard_map/all_to_all | solution.py:123
  53.3 13.1 %reshape.88 = f32[4096,4,8]{2,1,0:T(4,128)} reshape(f32[8,16384]{1,0:T(8,128)S(1)} %reduce.6) | data formatting | bytes 1048576
  66.4 6.7 %copy.96 = f32[8,4,8,512]{3,1,2,0:T(4,128)S(1)} copy(f32[8,4,8,512]{0,1,3,2:T(4,128)} %bitcast.216) | data formatting | bytes 1048576 | tf_op jit(solution)/shard_map/all_to_all | solution.py:123
  76.4 3.7 all-to-all-start.1
  80.4 28.5 %all-to-all-done.1 = f32[8,2,32,512]{3,0,1,2:T(8,128)S(1)} async-done(((f32[8,2,32,512]{3,0,1,2:T(8,128)}), f32[8,2,32,512]{3,0,1,2:T(8,128)S(1)}, u32[]{:S(2)}, u32[]{:S(2)}) %all-to-all-start.1) | async-done | bytes 1048608 | tf_op jit(solution)/shard_map/all_to_all | solution.py:130
  122.5 3.8 fusion.21
  135.1 11.1 %copy.110 = f32[2,8,4,4096]{1,2,0,3:T(4,128)} copy(f32[2,8,4,4096]{3,2,1,0:T(4,128)S(1)} %mul.315) | data formatting | bytes 2097152 | tf_op jit(solution)/shard_map/mul | solution.py:114
  146.2 14.5 %bitcast_bitcast_fusion = f32[4096,2,4,8]{3,2,1,0:T(4,128)} fusion(f32[2,8,4,4096]{1,2,0,3:T(4,128)} %copy.110), kind=kLoop, calls=%fused_computation.239 | loop fusion | bytes 2097152
  160.6 21.3 %reshape.89 = f32[8,1,32768]{2,1,0:T(1,128)S(1)} reshape(f32[4096,2,4,8]{3,2,1,0:T(4,128)} %bitcast_bitcast_fusion) | data formatting | bytes 2097152
  181.9 30.5 %all_to_all.106 = f32[8,1,32768]{2,1,0:T(1,128)S(1)} all-to-all(f32[8,1,32768]{2,1,0:T(1,128)S(1)} %reshape.89), channel_id=1, replica_groups=mesh['facet'=8,'chan'=32] {'facet'}, dimensions={0} | all-to-all | bytes 2097152 | tf_op jit(solution)/shard_map/all_to_all | solution.py:154
  212.4 3.1 reduce.7
  215.6 25.6 %reshape.90 = f32[4096,2,4,8]{3,2,1,0:T(4,128)} reshape(f32[8,32768]{1,0:T(8,128)S(1)} %reduce.7) | data formatting | bytes 2097152
  241.2 13.2 %copy.111 = f32[8,2,4,8,512]{4,2,3,0,1:T(4,128)S(1)} copy(f32[8,2,4,8,512]{0,2,1,4,3:T(4,128)} %bitcast.215) | data formatting | bytes 2097152 | tf_op jit(solution)/shard_map/all_to_all | solution.py:154
  257.2 3.5 all-to-all-start.3
  261.0 16.0 %all-to-all-done.3 = f32[8,32,512]{2,0,1:T(8,128)S(1)} async-done(((f32[8,32,512]{2,0,1:T(8,128)}), f32[8,32,512]{2,0,1:T(8,128)S(1)}, u32[]{:S(2)}, u32[]{:S(2)}) %all-to-all-start.3) | async-done | bytes 524320 | tf_op jit(solution)/shard_map/all_to_all | solution.py:159
  277.0 9.1 %all-to-all-start.4 = ((f32[256,4,128]{2,1,0:T(4,128)}), f32[256,4,128]{2,1,0:T(4,128)S(1)}, u32[]{:S(2)}, u32[]{:S(2)}) async-start(f32[256,4,128]{2,1,0:T(4,128)} %param.12), calls=%async_computation.4 | async-start | bytes 1048576 | tf_op jit(solution)/shard_map/all_to_all | solution.py:172
  286.2 2.2 collective-permute-start
  291.1 3.8 collective-permute-done.1
  294.9 2.7 all-to-all-done.4
  298.0 5.9 %copy.122 = f32[8,4,4096]{0,1,2:T(4,128)} copy(f32[8,4,4096]{2,0,1:T(8,128)S(1)} %get-tuple-element.76) | data formatting | bytes 1048576 | tf_op jit(solution)/shard_map/add | solution.py:177
  303.9 11.4 %reshape.91 = f32[32,1,4096]{2,1,0:T(1,128)S(1)} reshape(f32[4096,4,8]{2,1,0:T(4,128)} %bitcast.217) | data formatting | bytes 1048576
  315.4 17.2 %all_to_all.107 = f32[32,1,4096]{2,1,0:T(1,128)S(1)} all-to-all(f32[32,1,4096]{2,1,0:T(1,128)S(1)} %reshape.91), channel_id=1, replica_groups=mesh['facet'=8,'chan'=32] {'chan'}, dimensions={0} | all-to-all | bytes 1048576 | tf_op jit(solution)/shard_map/all_to_all | solution.py:179
  334.4 11.3 %reshape.92 = f32[4096,4,8]{2,1,0:T(4,128)} reshape(f32[32,4096]{1,0:T(8,128)S(1)} %reduce.8) | data formatting | bytes 1048576
  345.7 6.6 %copy.123 = f32[8,4,32,128]{3,0,2,1:T(8,128)S(1)} copy(f32[8,4,32,128]{0,1,3,2:T(4,128)} %bitcast.218) | data formatting | bytes 1048576 | tf_op jit(solution)/shard_map/all_to_all | solution.py:179
  353.4 105.1 %all-reduce.2.cloned.1.call-done = f32[256,128]{1,0:T(8,128)} async-done(((f32[256,128]{1,0:T(8,128)}), f32[256,128]{1,0:T(8,128)}) %all-reduce.2.cloned.1.call-update) | async-done | bytes 131088 | tf_op jit(solution)/shard_map/psum | solution.py:180
  460.1 11.7 %cholesky.22 = f32[128,128]{1,0:T(8,128)S(1)} custom-call(f32[128,128]{1,0:T(8,128)S(1)} %fusion.62), custom_call_target="Cholesky" | custom-call | tf_op jit(solution)/shard_map/jit(cholesky)/cholesky | solution.py:58
  473.2 9.8 %custom-call.7 = f32[1,128,128]{1,2,0:T(8,128)S(1)} custom-call(f32[1,128,128]{2,1,0:T(8,128)S(1)} %fusion.56), custom_call_target="InvertDiagBlocksLowerTriangular" | custom-call | tf_op jit(solution)/shard_map/jit(_solve_triangular)/triangular_solve | solution.py:59
  486.8 47.7 %all-gather.3.cloned.1.call-done = f32[4096,128]{1,0:T(8,128)} async-done(((f32[128,128]{1,0:T(8,128)}), f32[4096,128]{1,0:T(8,128)}) %all-gather.3.cloned.1.call-update) | async-done | bytes 2097168 | tf_op jit(solution)/shard_map/all_gather | solution.py:184
  538.9 5.4 while.23
  546.0 11.4 %while.24 = (s32[]{:T(128)}, f32[128,128]{0,1:T(8,128)S(1)}, f32[128,128]{1,0:T(8,128)S(1)}, s32[]{:T(128)}) while((s32[]{:T(128)}, f32[128,128]{0,1:T(8,128)S(1)}, f32[128,128]{1,0:T(8,128)S(1)}, s32[]{:T(128)}) %tuple.57), condition=%wide.region_10.11_spmd.clone, body=%wide.region_9.10_spmd.clone.sunk | while | flops 75563008 | bytes 852021 | solution.py:52
  (196 shorter events, 66.1 us)
Async XLA Ops:
  7.2 112.7 %copy-start = (f32[8,4,128,128]{3,2,1,0:T(8,128)S(1)}, f32[8,4,128,128]{3,2,1,0:T(8,128)}, u32[]{:S(2)}) copy-start(f32[8,4,128,128]{3,2,1,0:T(8,128)} %param.14) | copy-start | bytes 6291460
  66.4 13.8 %copy-start.7 = (s32[8,4]{0,1:T(4,128)S(1)}, s32[8,4]{0,1:T(4,128)}, u32[]{:S(2)}) copy-start(s32[8,4]{0,1:T(4,128)} %param.15) | copy-start | bytes 388
  66.4 13.8 %copy-start.8 = (s32[8,4]{0,1:T(4,128)S(1)}, s32[8,4]{0,1:T(4,128)}, u32[]{:S(2)}) copy-start(s32[8,4]{0,1:T(4,128)} %param.16) | copy-start | bytes 388
  76.4 32.5 %all-to-all-start.1 = ((f32[8,2,32,512]{3,0,1,2:T(8,128)}), f32[8,2,32,512]{3,0,1,2:T(8,128)S(1)}, u32[]{:S(2)}, u32[]{:S(2)}) async-start(f32[8,2,32,512]{3,0,1,2:T(8,128)} %copy.99), calls=%async_computation.1 | async-start | bytes 2097152 | tf_op jit(solution)/shard_map/all_to_all | solution.py:130
  114.2 7.5 %copy-start.5 = (f32[8,2,4,4,128]{4,3,2,1,0:T(4,128)S(1)}, f32[8,2,4,4,128]{4,3,2,1,0:T(4,128)}, u32[]{:S(2)}) copy-start(f32[8,2,4,4,128]{4,3,2,1,0:T(4,128)} %param.17) | copy-start | bytes 393220
  241.2 19.6 %copy-start.2 = (f32[8,4,4096]{2,1,0:T(4,128)S(1)}, f32[8,4,4096]{2,1,0:T(4,128)}, u32[]{:S(2)}) copy-start(f32[8,4,4096]{2,1,0:T(4,128)} %param.11) | copy-start | bytes 1572868
  257.2 19.8 %all-to-all-start.3 = ((f32[8,32,512]{2,0,1:T(8,128)}), f32[8,32,512]{2,0,1:T(8,128)S(1)}, u32[]{:S(2)}, u32[]{:S(2)}) async-start(f32[8,32,512]{2,0,1:T(8,128)} %copy.112), calls=%async_computation.3 | async-start | bytes 1048576 | tf_op jit(solution)/shard_map/all_to_all | solution.py:159
  277.0 20.6 %all-to-all-start.4 = ((f32[256,4,128]{2,1,0:T(4,128)}), f32[256,4,128]{2,1,0:T(4,128)S(1)}, u32[]{:S(2)}, u32[]{:S(2)}) async-start(f32[256,4,128]{2,1,0:T(4,128)} %param.12), calls=%async_computation.4 | async-start | bytes 1048576 | tf_op jit(solution)/shard_map/all_to_all | solution.py:172
  286.2 172.3 %all-reduce.2.cloned.1.call-start = ((), (), s32[]{:S(2)}) async-start(), calls=%async_computation.6 | async-start | bytes 262144 | tf_op jit(solution)/shard_map/psum | solution.py:180
  286.2 4.8 collective-permute-start
  288.5 6.4 %collective-permute-start.1 = (f32[8,1,4096]{2,0,1:T(8,128)S(1)}, f32[8,1,4096]{2,0,1:T(8,128)S(1)}, u32[]{:S(2)}, u32[]{:S(2)}) collective-permute-start(f32[8,1,4096]{2,0,1:T(8,128)S(1)} %get-tuple-element.85), channel_id=1, source_target_pairs={{32,0},{64,32},{96,64},{128,96},{160,128},{192,160},{224,192},{33,... | collective-permute-start | bytes 393224 | tf_op jit(solution)/shard_map/ppermute | solution.py:23
  334.4 17.9 %copy-start.6 = (bf16[4,128,128]{2,1,0:T(8,128)(2,1)S(1)}, bf16[4,128,128]{2,1,0:T(8,128)(2,1)}, u32[]{:S(2)}) copy-start(bf16[4,128,128]{2,1,0:T(8,128)(2,1)} %param.13) | copy-start | bytes 393220
  353.4 181.1 %all-gather.3.cloned.1.call-start = ((), (), s32[]{:S(2)}) async-start(), calls=%async_computation.7 | async-start | bytes 2162688 | tf_op jit(solution)/shard_map/all_gather | solution.py:184
  458.5 101.3 %copy-start.1 = (f32[8,4,128,128]{3,2,1,0:T(8,128)S(1)}, f32[8,4,128,128]{3,2,1,0:T(8,128)}, u32[]{:S(2)}) copy-start(f32[8,4,128,128]{3,2,1,0:T(8,128)} %param.14) | copy-start | bytes 6291460
  484.2 1.5 copy-start.3
  486.8 70.8 %copy-start.4 = (f32[128,256]{1,0:T(8,128)S(1)}, f32[128,256]{1,0:T(8,128)}, u32[]{:S(2)}) copy-start(f32[128,256]{1,0:T(8,128)} %copy-done.3) | copy-start | bytes 393220
Sparse Core Ops, SparseCore 0:
  353.5 104.9 all-reduce.1
  485.8 48.6 all-gather.2
